TPU v7x, 256 devices: a whole 4x4x8 slice. The times are simulated.
256 devices in a mesh: rep: 4 (over y), pipe: 8 (over z_lo, x), tp: 8 (over z_hi, core).
Axes of the slice: x: 4, y: 4, z: 8 (z_hi: 4, z_lo: 2; z = z_hi * 2 + z_lo), core: 2. Of those that a mesh axis runs over, the one named last changes fastest.
Arguments:
- act_forward: bfloat16 [8, 4, 128, 4096], P('pipe', 'rep', 'tp'), may hold values from -6 to 6
- act_saved: bfloat16 [8, 4, 128, 4096], P('pipe', 'rep', 'tp'), may hold values from -6 to 6
- grad_output: bfloat16 [8, 4, 128, 4096], P('pipe', 'rep', 'tp'), may hold values from -6 to 6
- norm_gain: bfloat16 [8, 4096], P('pipe'), may hold values from 0.099609375 to 1.8984375
- up_weight: bfloat16 [8, 4096, 14336], P('pipe', None, ('rep', 'tp')), may hold values from -0.09375 to 0.09375
- down_weight: bfloat16 [8, 14336, 4096], P('pipe', ('rep', 'tp')), may hold values from -0.046875 to 0.046875
- section_layers: int32 [4], replicated, may hold values from 1 to 3, 8 in all
- redirect_count: int32 [3, 4], replicated, may hold values from 0 to 3, as said below
- redirect_dest: int32 [3, 4], replicated, may hold values from 0 to 3, as said below
Outputs:
- arrive_forward: bfloat16 [8, 4, 128, 4096], P('pipe', 'rep', 'tp')
- arrive_backward: bfloat16 [8, 4, 128, 4096], P('pipe', 'rep', 'tp')
Inputs may be any that keep to these rules, and one draw needn't show every extreme that they name: `redirect_count`: counts are in blocks of 16 rows. At each boundary every replica either sends to another replica or has count zero; a sender's destination has count zero there, and each replica receives from at most one sender. Following the boundaries in order from 5 live blocks, every replica keeps at least one block and never holds more than 8. At the first boundary every sender sends to the replica 4 / 2 indices away (counted round); one replica sends exactly 3 blocks, filling its receiver to 8, and with four or more replicas another replica sends exactly one block. `redirect_dest`: the destination of a replica with count zero is the replica itself.
All inputs are finite; a program needn't handle non-finite values.
Results may differ from a plain program's by a relative error of at most 0.015.
Values may be sent and summed in bfloat16 or wider, within the bound.
No kernel may reach another device: no remote copies, remote signals or barrier semaphores. Data moves between devices by JAX's collectives and lax.ppermute only.
A program may use at most 128 MiB of HBM per device.

v0:
```python
import jax
import jax.numpy as jnp
from jax import lax
from jax.sharding import PartitionSpec as P

BLOCK = 16
CAPB = 8
START = 5


EPSILON = 1e-05


def from_behind(block, axis, distance):
    devices = range(lax.axis_size(axis))
    route = [(i - distance, i) for i in devices if i - distance in devices]
    return lax.ppermute(block, axis, route)


def moved_blocks(counts, dests, replica_ids):
    return jnp.where((dests != replica_ids) & (counts > 0), counts, 0)


def section_plan(section_layers, redirect_count, redirect_dest, segments, replicas):
    replica_ids = jnp.arange(replicas, dtype=jnp.int32)
    section_ends = (jnp.cumsum(section_layers) - 1)[:-1]
    positions = jnp.arange(segments, dtype=jnp.int32)
    matches = (section_ends[None, :] == positions[:, None]).astype(jnp.int32)
    segment_count = jnp.sum(matches[:, :, None] * redirect_count[None, :, :], axis=1)
    has_boundary = jnp.sum(matches, axis=1)[:, None]
    segment_dest = (
        jnp.sum(matches[:, :, None] * redirect_dest[None, :, :], axis=1)
        + (1 - has_boundary) * replica_ids[None, :]
    )
    live_list = [jnp.full((replicas,), START, jnp.int32)]
    for position in range(segments - 1):
        moved = moved_blocks(segment_count[position], segment_dest[position], replica_ids)
        incoming = jnp.sum(
            jnp.where(segment_dest[position][:, None] == replica_ids[None, :], moved[:, None], 0),
            axis=0,
        )
        live_list.append(live_list[-1] - moved + incoming)
    return (jnp.stack(live_list), segment_count, segment_dest)


def source_rows(live_before, counts, dests, replicas):
    replica_ids = jnp.arange(replicas, dtype=jnp.int32)
    block_ids = jnp.arange(CAPB, dtype=jnp.int32)
    moved = moved_blocks(counts, dests, replica_ids)
    sends = moved > 0
    same_dest = (
        (dests[None, :] == dests[:, None])
        & (replica_ids[None, :] < replica_ids[:, None])
        & sends[None, :]
    )
    kept = live_before - moved
    incoming = jnp.sum(
        jnp.where(sends[:, None] & (dests[:, None] == replica_ids[None, :]), moved[:, None], 0),
        axis=0,
    )
    offset = jnp.sum(jnp.where(same_dest, moved[None, :], 0), axis=1)
    hits = (
        sends[None, None, :]
        & (dests[None, None, :] == replica_ids[:, None, None])
        & (block_ids[None, :, None] >= offset[None, None, :])
        & (block_ids[None, :, None] < (offset + moved)[None, None, :])
    )
    from_block = (
        replica_ids[None, None, :] * CAPB + block_ids[None, :, None] - offset[None, None, :]
    )
    moved_source = jnp.sum(jnp.where(hits, from_block, 0), axis=2)
    own_local = block_ids[None, :] - incoming[:, None]
    own_ok = (own_local >= 0) & (own_local < kept[:, None])
    own_block = own_local + moved[:, None]
    source_block = jnp.where(
        jnp.any(hits, axis=2),
        moved_source,
        jnp.where(own_ok, replica_ids[:, None] * CAPB + own_block, -1),
    )
    row_ids = source_block[:, :, None] * BLOCK + jnp.arange(BLOCK, dtype=jnp.int32)[None, None, :]
    return jnp.where(source_block[:, :, None] >= 0, row_ids, -1).reshape(replicas * CAPB * BLOCK)


def inverse_rows(source):
    total = source.shape[0]
    target = jnp.where(source >= 0, source, total)
    return (
        jnp.full((total,), -1, jnp.int32)
        .at[target]
        .set(jnp.arange(total, dtype=jnp.int32), mode="drop")
    )


def pick_rows(values, index):
    taken = jnp.take(values, jnp.maximum(index, 0), axis=0)
    return jnp.where(index[:, None] >= 0, taken, jnp.zeros((), values.dtype))


def normalize(values, gain_row):
    wide = values.astype(jnp.float32)
    scale = lax.rsqrt(jnp.mean(wide * wide, axis=-1, keepdims=True) + EPSILON)
    return (wide * scale * gain_row.astype(jnp.float32)).astype(jnp.bfloat16)


def norm_back(values, gain_row, upstream):
    wide = values.astype(jnp.float32)
    scale = lax.rsqrt(jnp.mean(wide * wide, axis=-1, keepdims=True) + EPSILON)
    weighted = gain_row.astype(jnp.float32) * upstream
    return scale * weighted - wide * (scale * scale * scale) * jnp.mean(
        weighted * wide, axis=-1, keepdims=True
    )


def silu_slope(upper):
    sigma = jax.nn.sigmoid(upper)
    return sigma * (1.0 + upper * (1.0 - sigma))


def against_rows(left, right):
    return lax.dot_general(
        left, right, (((1,), (1,)), ((), ())), preferred_element_type=jnp.float32
    )


def route_rows(own_result, own_grad, later_mine, earlier_mine):
    every_result, every_grad = (
        lax.all_gather(own_result, ("rep", "tp"), axis=0, tiled=True),
        lax.all_gather(own_grad, ("rep", "tp"), axis=0, tiled=True),
    )
    return (pick_rows(every_result, later_mine), pick_rows(every_grad, earlier_mine))


def local(
    act_forward,
    act_saved,
    grad_output,
    norm_gain,
    up_weight,
    down_weight,
    section_layers,
    redirect_count,
    redirect_dest,
):
    segments = lax.axis_size("pipe")
    replicas = lax.axis_size("rep")
    splits = lax.axis_size("tp")
    segment_index = lax.axis_index("pipe")
    replica_index = lax.axis_index("rep")
    split_index = lax.axis_index("tp")
    fresh_own = act_forward[0, 0]
    saved_own = act_saved[0, 0]
    upstream_own = grad_output[0, 0]
    local_rows = fresh_own.shape[0]
    gain_row = norm_gain[0]
    w_up = up_weight[0]
    w_down = down_weight[0]
    live, segment_count, segment_dest = section_plan(
        section_layers, redirect_count, redirect_dest, segments, replicas
    )
    prior = jnp.maximum(segment_index - 1, 0)
    later = source_rows(
        live[segment_index], segment_count[segment_index], segment_dest[segment_index], replicas
    )
    earlier = inverse_rows(
        source_rows(live[prior], segment_count[prior], segment_dest[prior], replicas)
    )
    my_offset = (replica_index * splits + split_index) * local_rows
    later_mine = lax.dynamic_slice_in_dim(later, my_offset, local_rows)
    earlier_mine = lax.dynamic_slice_in_dim(earlier, my_offset, local_rows)
    fresh, saved, upstream = (
        lax.all_gather(fresh_own, ("rep", "tp"), axis=0, tiled=True),
        lax.all_gather(saved_own, ("rep", "tp"), axis=0, tiled=True),
        lax.all_gather(upstream_own, ("rep", "tp"), axis=0, tiled=True),
    )
    hidden = jax.nn.silu(
        jnp.dot(normalize(fresh, gain_row), w_up, preferred_element_type=jnp.float32)
    ).astype(jnp.bfloat16)
    upper = jnp.dot(normalize(saved, gain_row), w_up, preferred_element_type=jnp.float32)
    back_hidden = (against_rows(upstream, w_down) * silu_slope(upper)).astype(jnp.bfloat16)
    mixed = lax.psum_scatter(
        jnp.dot(hidden, w_down, preferred_element_type=jnp.float32).astype(jnp.bfloat16),
        ("rep", "tp"),
        scatter_dimension=0,
        tiled=True,
    ).astype(jnp.float32)
    returned = lax.psum_scatter(
        against_rows(back_hidden, w_up).astype(jnp.bfloat16),
        ("rep", "tp"),
        scatter_dimension=0,
        tiled=True,
    ).astype(jnp.float32)
    own_result = (fresh_own.astype(jnp.float32) + mixed).astype(jnp.bfloat16)
    own_grad = (upstream_own.astype(jnp.float32) + norm_back(saved_own, gain_row, returned)).astype(
        jnp.bfloat16
    )
    result, gradient = route_rows(own_result, own_grad, later_mine, earlier_mine)
    arrive_forward = from_behind(result, "pipe", 1)
    arrive_backward = from_behind(gradient, "pipe", -1)
    return (arrive_forward[None, None], arrive_backward[None, None])


def solution(mesh):
    in_specs = (
        P("pipe", "rep", "tp", None),
        P("pipe", "rep", "tp", None),
        P("pipe", "rep", "tp", None),
        P("pipe", None),
        P("pipe", None, ("rep", "tp")),
        P("pipe", ("rep", "tp"), None),
        P(),
        P(),
        P(),
    )
    out_specs = (P("pipe", "rep", "tp", None), P("pipe", "rep", "tp", None))
    return jax.shard_map(local, mesh=mesh, in_specs=in_specs, out_specs=out_specs, check_vma=False)
```

profile of v0, /device:TPU:32, one launch (start us, length us, event | category | flops | bytes accessed | tf_op | source)
XLA Modules:
  0.0 541.1 jit_solution(9313696484954163274)
XLA Ops:
  7.2 0.7 all-gather.17.cloned.1.call-update
  7.9 0.7 all-gather.15.cloned.1.call-update
  9.4 0.7 mul.229
  10.2 62.5 %all-gather.17.cloned.1.call-done = bf16[1,1,512,4096]{3,2,1,0:T(8,128)(2,1)} async-done(((bf16[1,1,16,4096]{3,2,1,0:T(8,128)(2,1)}), bf16[1,1,512,4096]{3,2,1,0:T(8,128)(2,1)}) %all-gather.17.cloned.1.call-update) | async-done | bytes 4194320 | tf_op jit(solution)/shard_map/all_gather | solution.py:172
  72.6 3.2 fusion.3
  76.1 4.2 fusion.6
  80.3 53.3 %all-gather.15.cloned.1.call-done = bf16[1,1,512,4096]{3,2,1,0:T(8,128)(2,1)} async-done(((bf16[1,1,16,4096]{3,2,1,0:T(8,128)(2,1)}), bf16[1,1,512,4096]{3,2,1,0:T(8,128)(2,1)}) %all-gather.15.cloned.1.call-update) | async-done | bytes 4194320 | tf_op jit(solution)/shard_map/all_gather | solution.py:173
  133.6 10.8 %convolution_convert_fusion = bf16[512,4096]{1,0:T(8,128)(2,1)} fusion(bf16[1,4096,448]{1,2,0:T(8,128)(2,1)} %param.15, bf16[1,448,4096]{2,1,0:T(8,128)(2,1)} %param.16, bf16[1,1,512,4096]{3,2,1,0:T(8,128)(2,1)} %all-gather.15.cloned.1.call-done, f32[512,448]{0,1:T(8,128)S(1)} %fusion.6), kind=kOutput, calls=%fused_computation.13 | convolution fusion | flops 3762257920 | bytes 16646144 | tf_op jit(solution)/shard_map/dot_general | solution.py:120
  144.7 49.9 %all-gather.13.cloned.1.call-done = bf16[1,1,512,4096]{3,2,1,0:T(8,128)(2,1)} async-done(((bf16[1,1,16,4096]{3,2,1,0:T(8,128)(2,1)}), bf16[1,1,512,4096]{3,2,1,0:T(8,128)(2,1)}) %all-gather.13.cloned.1.call-update) | async-done | bytes 4194320 | tf_op jit(solution)/shard_map/all_gather | solution.py:171
  194.6 3.1 fusion
  197.7 10.9 %convolution_convert_fusion.1 = bf16[512,4096]{1,0:T(8,128)(2,1)} fusion(bf16[1,448,4096]{2,1,0:T(8,128)(2,1)} %param.16, bf16[1,4096,448]{1,2,0:T(8,128)(2,1)} %param.15, bf16[1,1,512,4096]{3,2,1,0:T(8,128)(2,1)} %all-gather.13.cloned.1.call-done, f32[4096]{0:T(1024)S(1)} %bitcast.75, f32[512]{0:T(512)S(1)} %add_rsqrt_fusion.1), kind=kOutput, calls=%fused_computation.14 | convolution fusion | flops 3769729024 | bytes 15747072 | tf_op jit(solution)/shard_map/dot_general | solution.py:181
  208.7 87.2 %reduce-scatter.5.cloned.1.call-done = bf16[16,4096]{1,0:T(8,128)(2,1)} async-done(((bf16[512,4096]{1,0:T(8,128)(2,1)}), bf16[16,4096]{1,0:T(8,128)(2,1)}) %reduce-scatter.5.cloned.1.call-update) | async-done | bytes 131088 | tf_op jit(solution)/shard_map/reduce_scatter | solution.py:186
  295.9 1.1 fusion.47
  297.0 1.7 fusion.51
  299.8 97.2 %reduce-scatter.3.cloned.1.call-done = bf16[16,4096]{1,0:T(8,128)(2,1)} async-done(((bf16[512,4096]{1,0:T(8,128)(2,1)}), bf16[16,4096]{1,0:T(8,128)(2,1)}) %reduce-scatter.3.cloned.1.call-update) | async-done | bytes 131088 | tf_op jit(solution)/shard_map/reduce_scatter | solution.py:180
  397.0 1.6 fusion.53
  402.0 2.4 scatter_custom_fusion
  404.7 53.5 %all-gather.11.cloned.1.call-done = bf16[512,4096]{1,0:T(8,128)(2,1)} async-done(((bf16[16,4096]{1,0:T(8,128)(2,1)}), bf16[512,4096]{1,0:T(8,128)(2,1)}) %all-gather.11.cloned.1.call-update) | async-done | bytes 4194320 | tf_op jit(solution)/shard_map/all_gather | solution.py:128
  458.2 3.5 gather_fusion.1
  461.7 5.4 collective-permute-start.1
  467.1 52.6 %all-gather.9.cloned.1.call-done = bf16[512,4096]{1,0:T(8,128)(2,1)} async-done(((bf16[16,4096]{1,0:T(8,128)(2,1)}), bf16[512,4096]{1,0:T(8,128)(2,1)}) %all-gather.9.cloned.1.call-update) | async-done | bytes 4194320 | tf_op jit(solution)/shard_map/all_gather | solution.py:127
  519.7 3.5 gather_fusion
  523.3 3.4 collective-permute-start
  526.7 6.2 %collective-permute-done = bf16[16,4096]{1,0:T(8,128)(2,1)S(1)} collective-permute-done((bf16[16,4096]{1,0:T(8,128)(2,1)S(1)}, bf16[16,4096]{1,0:T(8,128)(2,1)S(1)}, u32[]{:S(2)}, u32[]{:S(2)}) %collective-permute-start) | collective-permute-done | bytes 131104 | tf_op jit(solution)/shard_map/ppermute | solution.py:17
  (100 shorter events, 7.4 us)
Async XLA Ops:
  7.2 65.5 %all-gather.17.cloned.1.call-start = ((), (), s32[]{:S(2)}) async-start(), calls=%async_computation.8 | async-start | bytes 4325376 | tf_op jit(solution)/shard_map/all_gather | solution.py:172
  7.9 125.7 %all-gather.15.cloned.1.call-start = ((), (), s32[]{:S(2)}) async-start(), calls=%async_computation.7 | async-start | bytes 4325376 | tf_op jit(solution)/shard_map/all_gather | solution.py:173
  8.6 186.0 %all-gather.13.cloned.1.call-start = ((), (), s32[]{:S(2)}) async-start(), calls=%async_computation.6 | async-start | bytes 4325376 | tf_op jit(solution)/shard_map/all_gather | solution.py:171
  9.4 286.5 %reduce-scatter.5.cloned.1.call-start = ((), (), s32[]{:S(2)}) async-start(), calls=%async_computation.4 | async-start | bytes 4325376 | tf_op jit(solution)/shard_map/reduce_scatter | solution.py:186
  72.6 3.4 copy-start
  144.5 252.4 %reduce-scatter.3.cloned.1.call-start = ((), (), s32[]{:S(2)}) async-start(), calls=%async_computation.2 | async-start | bytes 4325376 | tf_op jit(solution)/shard_map/reduce_scatter | solution.py:180
  208.6 87.3 %copy-start.1 = (bf16[1,1,16,4096]{3,2,1,0:T(8,128)(2,1)S(1)}, bf16[1,1,16,4096]{3,2,1,0:T(8,128)(2,1)}, u32[]{:S(2)}) copy-start(bf16[1,1,16,4096]{3,2,1,0:T(8,128)(2,1)} %param.12) | copy-start | bytes 393220
  208.6 88.4 %copy-start.2 = (bf16[1,1,16,4096]{3,2,1,0:T(8,128)(2,1)S(1)}, bf16[1,1,16,4096]{3,2,1,0:T(8,128)(2,1)}, u32[]{:S(2)}) copy-start(bf16[1,1,16,4096]{3,2,1,0:T(8,128)(2,1)} %param.13) | copy-start | bytes 393220
  208.6 90.2 %copy-start.6 = (s32[4]{0:T(128)S(1)}, s32[4]{0:T(128)}, u32[]{:S(2)}) copy-start(s32[4]{0:T(128)} %param.17) | copy-start | bytes 52
  208.6 90.5 %copy-start.4 = (s32[3,4]{1,0:T(4,128)S(1)}, s32[3,4]{1,0:T(4,128)}, u32[]{:S(2)}) copy-start(s32[3,4]{1,0:T(4,128)} %param.19) | copy-start | bytes 148
  208.6 90.5 %copy-start.5 = (s32[3,4]{1,0:T(4,128)S(1)}, s32[3,4]{1,0:T(4,128)}, u32[]{:S(2)}) copy-start(s32[3,4]{1,0:T(4,128)} %param.18) | copy-start | bytes 148
  208.6 188.3 %copy-start.3 = (bf16[1,1,16,4096]{3,2,1,0:T(8,128)(2,1)S(1)}, bf16[1,1,16,4096]{3,2,1,0:T(8,128)(2,1)}, u32[]{:S(2)}) copy-start(bf16[1,1,16,4096]{3,2,1,0:T(8,128)(2,1)} %param.11) | copy-start | bytes 393220
  208.7 249.5 %all-gather.11.cloned.1.call-start = ((), (), s32[]{:S(2)}) async-start(), calls=%async_computation.5 | async-start | bytes 4325376 | tf_op jit(solution)/shard_map/all_gather | solution.py:128
  298.7 221.0 %all-gather.9.cloned.1.call-start = ((), (), s32[]{:S(2)}) async-start(), calls=%async_computation.3 | async-start | bytes 4325376 | tf_op jit(solution)/shard_map/all_gather | solution.py:127
  461.7 65.0 %collective-permute-start.1 = (bf16[16,4096]{1,0:T(8,128)(2,1)S(1)}, bf16[16,4096]{1,0:T(8,128)(2,1)S(1)}, u32[]{:S(2)}, u32[]{:S(2)}) collective-permute-start(bf16[16,4096]{1,0:T(8,128)(2,1)S(1)} %select_select_fusion), channel_id=1, source_target_pairs={{8,0},{16,8},{24,16},{32,24},{40,32},{48,40},{56,48},{9,1},{17,9},... | collective-permute-start | bytes 393224 | tf_op jit(solution)/shard_map/ppermute | solution.py:17
  523.3 9.6 %collective-permute-start = (bf16[16,4096]{1,0:T(8,128)(2,1)S(1)}, bf16[16,4096]{1,0:T(8,128)(2,1)S(1)}, u32[]{:S(2)}, u32[]{:S(2)}) collective-permute-start(bf16[16,4096]{1,0:T(8,128)(2,1)S(1)} %select_select_fusion.1), channel_id=1, source_target_pairs={{0,8},{8,16},{16,24},{24,32},{32,40},{40,48},{48,56},{1,9},{9,17},... | collective-permute-start | bytes 393224 | tf_op jit(solution)/shard_map/ppermute | solution.py:17
Sparse Core Ops, SparseCore 0:
  10.5 62.0 all-gather.16
  75.2 58.3 all-gather.14
  136.2 58.4 all-gather.12
  198.4 97.4 reduce-scatter.4
  299.7 97.2 reduce-scatter.2
  399.9 58.1 all-gather.10
  461.3 58.4 all-gather.8
where the time goes:
time: 541 us
  waiting for transfers between devices  465 us (86%)
  matrix products  25.9 us (5%)
  other arithmetic  14.9 us (3%)
  between operations  14.4 us (3%)
  local copies, waits for them, and re-layouts  12.1 us (2%)
  starting transfers between devices  9.22 us (2%)
    reduce_scatter x1, waiting for transfers between devices, local(): lax.psum_scatter(jnp.dot(hidden, w_down, preferred_element_type=jnp.float...  97.2 us
    reduce_scatter x1, waiting for transfers between devices, local(): lax.psum_scatter(against_rows(back_hidden, w_up).astype(jnp.bfloat16), ('...  87.2 us
    all_gather x1, waiting for transfers between devices, local(): lax.all_gather(saved_own, ('rep', 'tp'), axis=0, tiled=True)  62.5 us
    all_gather x1, waiting for transfers between devices, route_rows(): lax.all_gather(own_grad, ('rep', 'tp'), axis=0, tiled=True)  53.5 us
    all_gather x1, waiting for transfers between devices, local(): lax.all_gather(upstream_own, ('rep', 'tp'), axis=0, tiled=True)  53.3 us
    all_gather x1, waiting for transfers between devices, route_rows(): lax.all_gather(own_result, ('rep', 'tp'), axis=0, tiled=True)  52.6 us
    all_gather x1, waiting for transfers between devices, local(): lax.all_gather(fresh_own, ('rep', 'tp'), axis=0, tiled=True)  49.9 us
    dot_general x1, matrix products, local(): jnp.dot(hidden, w_down, preferred_element_type=jnp.float32)  10.9 us
  transfers between devices with their start and end apart: 9, of which 8 were waited for; matrix products, arithmetic and copies ran while one was open for 9% of the time, Pallas kernels for 0%

commit v1 on v0

--- a/solution.py
+++ b/solution.py
@@ -91,11 +91,6 @@
     )
 
 
-def pick_rows(values, index):
-    taken = jnp.take(values, jnp.maximum(index, 0), axis=0)
-    return jnp.where(index[:, None] >= 0, taken, jnp.zeros((), values.dtype))
-
-
 def normalize(values, gain_row):
     wide = values.astype(jnp.float32)
     scale = lax.rsqrt(jnp.mean(wide * wide, axis=-1, keepdims=True) + EPSILON)
@@ -122,12 +117,16 @@
     )
 
 
-def route_rows(own_result, own_grad, later_mine, earlier_mine):
-    every_result, every_grad = (
-        lax.all_gather(own_result, ("rep", "tp"), axis=0, tiled=True),
-        lax.all_gather(own_grad, ("rep", "tp"), axis=0, tiled=True),
-    )
-    return (pick_rows(every_result, later_mine), pick_rows(every_grad, earlier_mine))
+def pick_blocks(values, blocks):
+    shaped = values.reshape(blocks.shape[0], BLOCK, values.shape[-1])
+    taken = jnp.take(shaped, jnp.maximum(blocks, 0), axis=0)
+    kept = jnp.where(blocks[:, None, None] >= 0, taken, jnp.zeros((), values.dtype))
+    return kept.reshape(values.shape)
+
+
+def row_blocks(rows):
+    heads = rows[::BLOCK]
+    return jnp.where(heads >= 0, heads // BLOCK, -1)
 
 
 def local(
@@ -147,10 +146,7 @@
     segment_index = lax.axis_index("pipe")
     replica_index = lax.axis_index("rep")
     split_index = lax.axis_index("tp")
-    fresh_own = act_forward[0, 0]
-    saved_own = act_saved[0, 0]
-    upstream_own = grad_output[0, 0]
-    local_rows = fresh_own.shape[0]
+    local_rows = act_forward.shape[2]
     gain_row = norm_gain[0]
     w_up = up_weight[0]
     w_down = down_weight[0]
@@ -158,20 +154,20 @@
         section_layers, redirect_count, redirect_dest, segments, replicas
     )
     prior = jnp.maximum(segment_index - 1, 0)
-    later = source_rows(
-        live[segment_index], segment_count[segment_index], segment_dest[segment_index], replicas
-    )
-    earlier = inverse_rows(
-        source_rows(live[prior], segment_count[prior], segment_dest[prior], replicas)
+    later = row_blocks(
+        source_rows(
+            live[segment_index], segment_count[segment_index], segment_dest[segment_index], replicas
+        )
+    )
+    earlier = row_blocks(
+        inverse_rows(source_rows(live[prior], segment_count[prior], segment_dest[prior], replicas))
     )
     my_offset = (replica_index * splits + split_index) * local_rows
-    later_mine = lax.dynamic_slice_in_dim(later, my_offset, local_rows)
-    earlier_mine = lax.dynamic_slice_in_dim(earlier, my_offset, local_rows)
-    fresh, saved, upstream = (
-        lax.all_gather(fresh_own, ("rep", "tp"), axis=0, tiled=True),
-        lax.all_gather(saved_own, ("rep", "tp"), axis=0, tiled=True),
-        lax.all_gather(upstream_own, ("rep", "tp"), axis=0, tiled=True),
-    )
+    own = jnp.stack([act_forward[0, 0], act_saved[0, 0], grad_output[0, 0]])
+    every = lax.all_gather(own, ("rep", "tp"), axis=1, tiled=True)
+    fresh = pick_blocks(every[0], later)
+    saved = pick_blocks(every[1], earlier)
+    upstream = pick_blocks(every[2], earlier)
     hidden = jax.nn.silu(
         jnp.dot(normalize(fresh, gain_row), w_up, preferred_element_type=jnp.float32)
     ).astype(jnp.bfloat16)
@@ -189,11 +185,13 @@
         scatter_dimension=0,
         tiled=True,
     ).astype(jnp.float32)
-    own_result = (fresh_own.astype(jnp.float32) + mixed).astype(jnp.bfloat16)
-    own_grad = (upstream_own.astype(jnp.float32) + norm_back(saved_own, gain_row, returned)).astype(
-        jnp.bfloat16
-    )
-    result, gradient = route_rows(own_result, own_grad, later_mine, earlier_mine)
+    fresh_mine = lax.dynamic_slice_in_dim(fresh, my_offset, local_rows)
+    saved_mine = lax.dynamic_slice_in_dim(saved, my_offset, local_rows)
+    upstream_mine = lax.dynamic_slice_in_dim(upstream, my_offset, local_rows)
+    result = (fresh_mine.astype(jnp.float32) + mixed).astype(jnp.bfloat16)
+    gradient = (
+        upstream_mine.astype(jnp.float32) + norm_back(saved_mine, gain_row, returned)
+    ).astype(jnp.bfloat16)
     arrive_forward = from_behind(result, "pipe", 1)
     arrive_backward = from_behind(gradient, "pipe", -1)
     return (arrive_forward[None, None], arrive_backward[None, None])

time: 541 us -> 370 us (0.68)
  waiting for transfers between devices: 465 us -> 266 us
  local copies, waits for them, and re-layouts: 12.1 us -> 29.4 us
  other arithmetic: 14.9 us -> 25.4 us
    all_gather x5 -> x1, waiting for transfers between devices: 272 us -> 92.7 us  [local(): every = lax.all_gather(own, ('rep', 'tp'), axis=1, tiled=True)]
    reduce_scatter x1, waiting for transfers between devices: 97.2 us -> 73.4 us  [local(): lax.psum_scatter(jnp.dot(hidden, w_down, preferred_element_type=jnp.float...]
    reduce_scatter x1, waiting for transfers between devices: 87.2 us -> 96.9 us  [local(): lax.psum_scatter(against_rows(back_hidden, w_up).astype(jnp.bfloat16), ('...]
    slice x0 -> x3, local copies, waits for them, and re-layouts: none -> 9.08 us  [the longest x1 8.83 us: local(): saved = pick_blocks(every[1], earlier)]
    gather x2 -> x3, local copies, waits for them, and re-layouts: 6.95 us -> 14.9 us  [pick_blocks(): taken = jnp.take(shaped, jnp.maximum(blocks, 0), axis=0)]
    dot_general x1, matrix products: 10.9 us -> 4.35 us  [local(): jnp.dot(hidden, w_down, preferred_element_type=jnp.float32)]
  transfers between devices with their start and end apart: 9 -> 5, of which waited for: 8 -> 4; matrix products, arithmetic and copies ran while one was open for 9% -> 10% of each run, Pallas kernels for 0% -> 0%
where the time goes in v1:
time: 370 us; the launch traced here: 367 us
  waiting for transfers between devices  266 us (72%)
  local copies, waits for them, and re-layouts  29.4 us (8%)
  other arithmetic  25.4 us (7%)
  matrix products  23.2 us (6%)
  between operations  14.1 us (4%)
  starting transfers between devices  9.35 us (3%)
    reduce_scatter x1, waiting for transfers between devices, local(): lax.psum_scatter(against_rows(back_hidden, w_up).astype(jnp.bfloat16), ('...  96.9 us
    all_gather x1, waiting for transfers between devices, local(): every = lax.all_gather(own, ('rep', 'tp'), axis=1, tiled=True)  92.7 us
    reduce_scatter x1, waiting for transfers between devices, local(): lax.psum_scatter(jnp.dot(hidden, w_down, preferred_element_type=jnp.float...  73.4 us
    gather x3, local copies, waits for them, and re-layouts, pick_blocks(): taken = jnp.take(shaped, jnp.maximum(blocks, 0), axis=0)  14.9 us
    dot_general x1, matrix products, against_rows(): lax.dot_general(left, right, (((1,), (1,)), ((), ())), preferred_element_...  11.1 us
    ppermute x2, starting transfers between devices, from_behind(): return lax.ppermute(block, axis, route)  9.05 us
    slice x1, local copies, waits for them, and re-layouts, local(): saved = pick_blocks(every[1], earlier)  8.83 us
    reduce_sum x2, other arithmetic, normalize(): scale = lax.rsqrt(jnp.mean(wide * wide, axis=-1, keepdims=True) + EPSILON)  8.13 us
  transfers between devices with their start and end apart: 5, of which 4 were waited for; matrix products, arithmetic and copies ran while one was open for 10% of the time, Pallas kernels for 0%

profile of v1, /device:TPU:32, one launch (start us, length us, event | category | flops | bytes accessed | tf_op | source)
XLA Modules:
  0.0 367.0 jit_solution(12531829389518307346)
XLA Ops:
  7.2 1.9 pad_maximum_fusion
  9.1 0.8 reduce-window.9
  14.7 2.4 scatter_custom_fusion
  18.5 92.7 %all-gather.2.cloned.1.call-done = bf16[3,512,4096]{2,1,0:T(8,128)(2,1)} async-done(((bf16[3,16,4096]{2,1,0:T(8,128)(2,1)}), bf16[3,512,4096]{2,1,0:T(8,128)(2,1)}) %all-gather.2.cloned.1.call-update) | async-done | bytes 12582928 | tf_op jit(solution)/shard_map/all_gather | solution.py:167
  111.2 8.8 %fusion.75 = (bf16[1,512,4096]{2,1,0:T(8,128)(2,1)}, bf16[1,512,4096]{2,1,0:T(8,128)(2,1)}, bf16[1,512,4096]{2,1,0:T(8,128)(2,1)}) fusion(bf16[3,512,4096]{2,1,0:T(8,128)(2,1)} %all-gather.2.cloned.1.call-done), kind=kLoop, calls=%fused_computation.211 | loop fusion | bytes 25165824 | tf_op jit(solution)/shard_map/slice | solution.py:169
  120.0 5.0 %gather_fusion.2 = bf16[32,16,4096]{2,1,0:T(8,128)(2,1)} fusion(bf16[32,16,4096]{2,1,0:T(8,128)(2,1)} %bitcast.54, s32[1024]{0:T(1024)S(1)} %pad_clamp_fusion), kind=kCustom, calls=%fused_computation.2.clone | custom fusion | bytes 8388736 | tf_op jit(solution)/shard_map/jit(_take)/gather | solution.py:122
  125.0 4.6 %fusion.3 = (f32[32,16]{1,0:T(8,128)S(1)}, bf16[32,16,4096]{2,1,0:T(8,128)(2,1)}) fusion(bf16[32,16,4096]{2,1,0:T(8,128)(2,1)} %gather_fusion.2, pred[32]{0:T(512)(128)(4,1)S(1)} %broadcast_compare_fusion.2, pred[32]{0:T(512)(128)(4,1)S(1)} %get-tuple-element.37), kind=kLoop, calls=%fused_computation.11 | loop fusion | flops 10485248 | bytes 8390720 | tf_op jit(solution)/shard_map/reduce_sum | solution.py:96
  129.6 5.0 %gather_fusion = bf16[32,16,4096]{2,1,0:T(8,128)(2,1)} fusion(bf16[32,16,4096]{2,1,0:T(8,128)(2,1)} %bitcast.53, s32[1024]{0:T(1024)S(1)} %pad_clamp_fusion.1), kind=kCustom, calls=%fused_computation.clone | custom fusion | bytes 8388736 | tf_op jit(solution)/shard_map/jit(_take)/gather | solution.py:122
  134.6 3.5 fusion
  138.2 4.2 %fusion.5 = (bf16[32,16,4096]{2,1,0:T(8,128)(2,1)}, bf16[32,16,4096]{2,1,0:T(8,128)(2,1)S(1)}) fusion(bf16[32,16,4096]{2,1,0:T(8,128)(2,1)S(1)} %copy-done, f32[32,16]{1,0:T(8,128)S(1)} %add_rsqrt_fusion, f32[4096]{0:T(1024)S(1)} %bitcast.59, f32[32,16]{1,0:T(8,128)S(1)} %add_rsqrt_fusion.1, bf16[32,16,4096]{2,1,0:T(8,128)(2,1)S(1)} %get-tuple-element.44), kind=kLoop, calls=%fused_computation.13 | loop fusion | flops 16777216 | bytes 16797696 | tf_op jit(solution)/shard_map/convert_element_type | solution.py:97
  142.9 2.2 multiply_convert_fusion
  145.2 4.3 %convolution_convert_fusion.1 = bf16[512,4096]{1,0:T(8,128)(2,1)} fusion(bf16[512,448]{0,1:T(8,128)(2,1)S(1)} %multiply_convert_fusion, bf16[1,448,4096]{2,1,0:T(8,128)(2,1)S(1)} %copy-done.3), kind=kOutput, calls=%fused_computation.15 | convolution fusion | flops 1881145344 | bytes 8323072 | tf_op jit(solution)/shard_map/dot_general | solution.py:177
  149.8 4.9 %gather_fusion.1 = bf16[32,16,4096]{2,1,0:T(8,128)(2,1)} fusion(bf16[32,16,4096]{2,1,0:T(8,128)(2,1)} %bitcast.52, s32[1024]{0:T(1024)S(1)} %pad_clamp_fusion), kind=kCustom, calls=%fused_computation.1.clone | custom fusion | bytes 8388736 | tf_op jit(solution)/shard_map/jit(_take)/gather | solution.py:122
  154.7 5.5 %fusion.10 = f32[512,448]{0,1:T(8,128)S(1)} fusion(bf16[512,4096]{1,0:T(8,128)(2,1)} %bitcast.57, bf16[1,4096,448]{1,2,0:T(8,128)(2,1)} %param.15), kind=kOutput, calls=%fused_computation.23 | convolution fusion | flops 1879048192 | bytes 8781824 | tf_op jit(solution)/shard_map/dot_general | solution.py:174
  160.3 2.5 select_select_fusion.1
  162.8 11.1 %convolution_convert_fusion = bf16[512,4096]{1,0:T(8,128)(2,1)} fusion(bf16[1,4096,448]{1,2,0:T(8,128)(2,1)} %param.15, bf16[512,4096]{1,0:T(8,128)(2,1)} %bitcast.55, bf16[1,448,4096]{2,1,0:T(8,128)(2,1)} %param.16, f32[512,448]{0,1:T(8,128)S(1)} %fusion.10), kind=kOutput, calls=%fused_computation.14 | convolution fusion | flops 3762257920 | bytes 16646144 | tf_op jit(solution)/shard_map/dot_general | solution.py:115
  173.9 73.4 %reduce-scatter.3.cloned.1.call-done = bf16[16,4096]{1,0:T(8,128)(2,1)} async-done(((bf16[512,4096]{1,0:T(8,128)(2,1)}), bf16[16,4096]{1,0:T(8,128)(2,1)}) %reduce-scatter.3.cloned.1.call-update) | async-done | bytes 131088 | tf_op jit(solution)/shard_map/reduce_scatter | solution.py:176
  247.4 1.0 add_convert_fusion
  248.4 3.3 collective-permute-start
  251.7 96.9 %reduce-scatter.5.cloned.1.call-done = bf16[16,4096]{1,0:T(8,128)(2,1)} async-done(((bf16[512,4096]{1,0:T(8,128)(2,1)}), bf16[16,4096]{1,0:T(8,128)(2,1)}) %reduce-scatter.5.cloned.1.call-update) | async-done | bytes 131088 | tf_op jit(solution)/shard_map/reduce_scatter | solution.py:182
  348.6 1.1 fusion.25
  349.7 1.2 fusion.29
  350.9 5.7 %collective-permute-start.1 = (bf16[16,4096]{1,0:T(8,128)(2,1)S(1)}, bf16[16,4096]{1,0:T(8,128)(2,1)S(1)}, u32[]{:S(2)}, u32[]{:S(2)}) collective-permute-start(bf16[16,4096]{1,0:T(8,128)(2,1)S(1)} %fusion.29), channel_id=1, source_target_pairs={{8,0},{16,8},{24,16},{32,24},{40,32},{48,40},{56,48},{9,1},{17,9},... | collective-permute-start | bytes 393224 | tf_op jit(solution)/shard_map/ppermute | solution.py:17
  356.6 2.5 collective-permute-done.1
  (95 shorter events, 8.1 us)
Async XLA Ops:
  7.2 104.0 %all-gather.2.cloned.1.call-start = ((), (), s32[]{:S(2)}) async-start(), calls=%async_computation.2 | async-start | bytes 12976128 | tf_op jit(solution)/shard_map/all_gather | solution.py:167
  9.1 238.3 %reduce-scatter.3.cloned.1.call-start = ((), (), s32[]{:S(2)}) async-start(), calls=%async_computation.3 | async-start | bytes 4325376 | tf_op jit(solution)/shard_map/reduce_scatter | solution.py:176
  134.6 3.6 copy-start
  138.1 4.3 %copy-start.1 = (bf16[32,16,4096]{2,1,0:T(8,128)(2,1)}, bf16[32,16,4096]{2,1,0:T(8,128)(2,1)S(1)}, u32[]{:S(2)}) copy-start(bf16[32,16,4096]{2,1,0:T(8,128)(2,1)S(1)} %get-tuple-element.44) | copy-start | bytes 12582916
  138.2 4.8 %copy-start.4 = (bf16[1,4096,448]{1,2,0:T(8,128)(2,1)S(1)}, bf16[1,4096,448]{1,2,0:T(8,128)(2,1)}, u32[]{:S(2)}) copy-start(bf16[1,4096,448]{1,2,0:T(8,128)(2,1)} %param.15) | copy-start | bytes 11010052
  142.9 2.2 copy-start.3
  149.5 199.0 %reduce-scatter.5.cloned.1.call-start = ((), (), s32[]{:S(2)}) async-start(), calls=%async_computation.4 | async-start | bytes 4325376 | tf_op jit(solution)/shard_map/reduce_scatter | solution.py:182
  154.7 5.5 %copy-start.2 = (bf16[32,16,4096]{2,1,0:T(8,128)(2,1)S(1)}, bf16[32,16,4096]{2,1,0:T(8,128)(2,1)}, u32[]{:S(2)}) copy-start(bf16[32,16,4096]{2,1,0:T(8,128)(2,1)} %gather_fusion.1) | copy-start | bytes 12582916
  248.4 108.3 %collective-permute-start = (bf16[16,4096]{1,0:T(8,128)(2,1)S(1)}, bf16[16,4096]{1,0:T(8,128)(2,1)S(1)}, u32[]{:S(2)}, u32[]{:S(2)}) collective-permute-start(bf16[16,4096]{1,0:T(8,128)(2,1)S(1)} %add_convert_fusion), channel_id=1, source_target_pairs={{0,8},{8,16},{16,24},{24,32},{32,40},{40,48},{48,56},{1,9},{9,17},... | collective-permute-start | bytes 393224 | tf_op jit(solution)/shard_map/ppermute | solution.py:17
  350.9 8.2 %collective-permute-start.1 = (bf16[16,4096]{1,0:T(8,128)(2,1)S(1)}, bf16[16,4096]{1,0:T(8,128)(2,1)S(1)}, u32[]{:S(2)}, u32[]{:S(2)}) collective-permute-start(bf16[16,4096]{1,0:T(8,128)(2,1)S(1)} %fusion.29), channel_id=1, source_target_pairs={{8,0},{16,8},{24,16},{32,24},{40,32},{48,40},{56,48},{9,1},{17,9},... | collective-permute-start | bytes 393224 | tf_op jit(solution)/shard_map/ppermute | solution.py:17
Sparse Core Ops, SparseCore 0:
  10.6 100.5 all-gather.1
  149.7 97.6 reduce-scatter.2
  251.3 97.2 reduce-scatter.4

commit v2 on v1

--- a/solution.py
+++ b/solution.py
@@ -1,7 +1,7 @@
 import jax
 import jax.numpy as jnp
 from jax import lax
-from jax.sharding import PartitionSpec as P
+from jax.sharding import Mesh, PartitionSpec as P
 
 BLOCK = 16
 CAPB = 8
@@ -118,15 +118,34 @@
 
 
 def pick_blocks(values, blocks):
-    shaped = values.reshape(blocks.shape[0], BLOCK, values.shape[-1])
+    shaped = values.reshape(-1, BLOCK, values.shape[-1])
     taken = jnp.take(shaped, jnp.maximum(blocks, 0), axis=0)
     kept = jnp.where(blocks[:, None, None] >= 0, taken, jnp.zeros((), values.dtype))
-    return kept.reshape(values.shape)
+    return kept.reshape(-1, values.shape[-1])
 
 
 def row_blocks(rows):
     heads = rows[::BLOCK]
     return jnp.where(heads >= 0, heads // BLOCK, -1)
+
+
+def swap_cores(values):
+    return lax.ppermute(values, "core", [(0, 1), (1, 0)])
+
+
+def gathered_place(blocks, cores, core_index, per_core):
+    split = blocks % (cores * per_core)
+    spot = (split % cores != core_index) * (lax.axis_size("rep") * per_core)
+    spot = spot + (blocks // (cores * per_core)) * per_core + split // cores
+    return jnp.where(blocks >= 0, spot, -1)
+
+
+def two_stage_sum(partial, half):
+    mine, theirs = partial[:half], partial[half:]
+    total = (mine.astype(jnp.float32) + swap_cores(theirs).astype(jnp.float32)).astype(jnp.bfloat16)
+    return lax.psum_scatter(total, ("rep", "zh"), scatter_dimension=0, tiled=True).astype(
+        jnp.float32
+    )
 
 
 def local(
@@ -142,10 +161,12 @@
 ):
     segments = lax.axis_size("pipe")
     replicas = lax.axis_size("rep")
-    splits = lax.axis_size("tp")
+    per_core = lax.axis_size("zh")
+    cores = lax.axis_size("core")
     segment_index = lax.axis_index("pipe")
     replica_index = lax.axis_index("rep")
-    split_index = lax.axis_index("tp")
+    zh_index = lax.axis_index("zh")
+    core_index = lax.axis_index("core")
     local_rows = act_forward.shape[2]
     gain_row = norm_gain[0]
     w_up = up_weight[0]
@@ -162,32 +183,35 @@
     earlier = row_blocks(
         inverse_rows(source_rows(live[prior], segment_count[prior], segment_dest[prior], replicas))
     )
-    my_offset = (replica_index * splits + split_index) * local_rows
+    group = replicas * per_core
+    slots = jnp.arange(cores * group, dtype=jnp.int32)
+    slot_core = jnp.where(slots < group, core_index, cores - 1 - core_index)
+    slot_group = slots % group
+    dest = (slot_group // per_core) * (per_core * cores) + (slot_group % per_core) * cores + slot_core
+    me = replica_index * (per_core * cores) + zh_index * cores + core_index
+    later_at = gathered_place(later, cores, core_index, per_core)
+    earlier_at = gathered_place(earlier, cores, core_index, per_core)
     own = jnp.stack([act_forward[0, 0], act_saved[0, 0], grad_output[0, 0]])
-    every = lax.all_gather(own, ("rep", "tp"), axis=1, tiled=True)
-    fresh = pick_blocks(every[0], later)
-    saved = pick_blocks(every[1], earlier)
-    upstream = pick_blocks(every[2], earlier)
+    near = lax.all_gather(own, ("rep", "zh"), axis=1, tiled=True)
+    every = jnp.concatenate([near, swap_cores(near)], axis=1)
     hidden = jax.nn.silu(
-        jnp.dot(normalize(fresh, gain_row), w_up, preferred_element_type=jnp.float32)
+        jnp.dot(normalize(every[0], gain_row), w_up, preferred_element_type=jnp.float32)
     ).astype(jnp.bfloat16)
-    upper = jnp.dot(normalize(saved, gain_row), w_up, preferred_element_type=jnp.float32)
-    back_hidden = (against_rows(upstream, w_down) * silu_slope(upper)).astype(jnp.bfloat16)
-    mixed = lax.psum_scatter(
-        jnp.dot(hidden, w_down, preferred_element_type=jnp.float32).astype(jnp.bfloat16),
-        ("rep", "tp"),
-        scatter_dimension=0,
-        tiled=True,
-    ).astype(jnp.float32)
-    returned = lax.psum_scatter(
-        against_rows(back_hidden, w_up).astype(jnp.bfloat16),
-        ("rep", "tp"),
-        scatter_dimension=0,
-        tiled=True,
-    ).astype(jnp.float32)
-    fresh_mine = lax.dynamic_slice_in_dim(fresh, my_offset, local_rows)
-    saved_mine = lax.dynamic_slice_in_dim(saved, my_offset, local_rows)
-    upstream_mine = lax.dynamic_slice_in_dim(upstream, my_offset, local_rows)
+    upper = jnp.dot(normalize(every[1], gain_row), w_up, preferred_element_type=jnp.float32)
+    back_hidden = (against_rows(every[2], w_down) * silu_slope(upper)).astype(jnp.bfloat16)
+    half = group * local_rows
+    mixed = two_stage_sum(
+        jnp.dot(pick_blocks(hidden, later_at[dest]), w_down, preferred_element_type=jnp.float32).astype(
+            jnp.bfloat16
+        ),
+        half,
+    )
+    returned = two_stage_sum(
+        against_rows(pick_blocks(back_hidden, earlier_at[dest]), w_up).astype(jnp.bfloat16), half
+    )
+    fresh_mine = pick_blocks(every[0], later_at[me][None])
+    saved_mine = pick_blocks(every[1], earlier_at[me][None])
+    upstream_mine = pick_blocks(every[2], earlier_at[me][None])
     result = (fresh_mine.astype(jnp.float32) + mixed).astype(jnp.bfloat16)
     gradient = (
         upstream_mine.astype(jnp.float32) + norm_back(saved_mine, gain_row, returned)
@@ -198,16 +222,23 @@
 
 
 def solution(mesh):
+    cores = 2
+    shape = mesh.devices.shape
+    fine = Mesh(
+        mesh.devices.reshape(shape[0], shape[1], shape[2] // cores, cores),
+        ("rep", "pipe", "zh", "core"),
+    )
+    rows = P("pipe", "rep", ("zh", "core"), None)
     in_specs = (
-        P("pipe", "rep", "tp", None),
-        P("pipe", "rep", "tp", None),
-        P("pipe", "rep", "tp", None),
+        rows,
+        rows,
+        rows,
         P("pipe", None),
-        P("pipe", None, ("rep", "tp")),
-        P("pipe", ("rep", "tp"), None),
+        P("pipe", None, ("rep", "zh", "core")),
+        P("pipe", ("rep", "zh", "core"), None),
         P(),
         P(),
         P(),
     )
-    out_specs = (P("pipe", "rep", "tp", None), P("pipe", "rep", "tp", None))
-    return jax.shard_map(local, mesh=mesh, in_specs=in_specs, out_specs=out_specs, check_vma=False)
+    out_specs = (rows, rows)
+    return jax.shard_map(local, mesh=fine, in_specs=in_specs, out_specs=out_specs, check_vma=False)

time: 370 us -> 347 us (0.938)
  waiting for transfers between devices: 266 us -> 251 us
  other arithmetic: 25.4 us -> 18.5 us
  matrix products: 23.2 us -> 18.8 us
    reduce_scatter x2, waiting for transfers between devices: 170 us -> 140 us  [two_stage_sum(): lax.psum_scatter(total, ('rep', 'zh'), scatter_dimension=0, tiled=True)]
    gather x3 -> x2, local copies, waits for them, and re-layouts: 14.9 us -> 1.16 us  [pick_blocks(): taken = jnp.take(shaped, jnp.maximum(blocks, 0), axis=0)]
    unnamed x12 -> x11, local copies, waits for them, and re-layouts: 1.83 us -> 10 us
    ppermute x0 -> x3, waiting for transfers between devices: none -> 8.03 us  [swap_cores(): return lax.ppermute(values, 'core', [(0, 1), (1, 0)])]
    reduce_sum x2 -> x1, other arithmetic: 8.13 us -> 1.8 us  [normalize(): scale = lax.rsqrt(jnp.mean(wide * wide, axis=-1, keepdims=True) + EPSILON)]
    dot_general x1 -> x2, matrix products: 11.1 us -> 6.61 us  [against_rows(): lax.dot_general(left, right, (((1,), (1,)), ((), ())), preferred_element_...]
    all_gather x1, waiting for transfers between devices: 92.7 us -> 97.1 us  [local(): near = lax.all_gather(own, ('rep', 'zh'), axis=1, tiled=True)]
    slice x1 -> x3, local copies, waits for them, and re-layouts: 8.83 us -> 10.8 us  [the longest x1 9.14 us: local(): saved_mine = pick_blocks(every[1], earlier_at[me][None])]
  transfers between devices with their start and end apart: 5 -> 8, of which waited for: 4 -> 7; matrix products, arithmetic and copies ran while one was open for 10% -> 12% of each run, Pallas kernels for 0% -> 0%
where the time goes in v2:
time: 347 us
  waiting for transfers between devices  251 us (72%)
  local copies, waits for them, and re-layouts  32.1 us (9%)
  matrix products  18.8 us (5%)
  other arithmetic  18.5 us (5%)
  between operations  16.7 us (5%)
  starting transfers between devices  9.77 us (3%)
    reduce_scatter x2, waiting for transfers between devices, two_stage_sum(): lax.psum_scatter(total, ('rep', 'zh'), scatter_dimension=0, tiled=True)  140 us
    all_gather x1, waiting for transfers between devices, local(): near = lax.all_gather(own, ('rep', 'zh'), axis=1, tiled=True)  97.1 us
    unnamed x11, local copies, waits for them, and re-layouts  10 us
    ppermute x2, starting transfers between devices, from_behind(): return lax.ppermute(block, axis, route)  9.28 us
    slice x1, local copies, waits for them, and re-layouts, local(): saved_mine = pick_blocks(every[1], earlier_at[me][None])  9.14 us
    ppermute x3, waiting for transfers between devices, swap_cores(): return lax.ppermute(values, 'core', [(0, 1), (1, 0)])  8.03 us
  transfers between devices with their start and end apart: 8, of which 7 were waited for; matrix products, arithmetic and copies ran while one was open for 12% of the time, Pallas kernels for 0%

profile of v2, /device:TPU:32, one launch (start us, length us, event | category | flops | bytes accessed | tf_op | source)
XLA Modules:
  0.0 346.9 jit_solution(16940741597355871412)
XLA Ops:
  7.2 1.8 pad_maximum_fusion
  12.4 97.1 %all-gather.2.cloned.1.call-done = bf16[3,256,4096]{2,1,0:T(8,128)(2,1)} async-done(((bf16[3,16,4096]{2,1,0:T(8,128)(2,1)}), bf16[3,256,4096]{2,1,0:T(8,128)(2,1)}) %all-gather.2.cloned.1.call-update) | async-done | bytes 6291472 | tf_op jit(solution)/shard_map/all_gather | solution.py:195
  111.8 2.4 scatter_custom_fusion
  115.9 3.2 constant_dynamic-update-slice_fusion.1
  120.0 3.2 constant_dynamic-update-slice_fusion
  123.2 1.8 fusion.3
  125.1 3.0 copy-done.2
  128.0 2.2 fusion.7
  130.8 2.2 fusion.28
  134.0 4.4 %convolution_convert_fusion = bf16[512,4096]{1,0:T(8,128)(2,1)S(1)} fusion(bf16[512,448]{1,0:T(8,128)(2,1)S(1)} %bitcast.86, bf16[1,4096,448]{1,2,0:T(8,128)(2,1)} %param.17), kind=kOutput, calls=%fused_computation.15 | convolution fusion | flops 1881145344 | bytes 8323072 | tf_op jit(solution)/shard_map/dot_general | solution.py:115
  138.4 1.9 copy-done.1
  140.4 1.6 slice.133
  143.1 3.2 collective-permute-done.3
  146.3 3.7 %add_convert_fusion = bf16[256,4096]{1,0:T(8,128)(2,1)} fusion(bf16[256,4096]{1,0:T(8,128)(2,1)S(1)} %collective-permute-done.3, bf16[512,4096]{1,0:T(8,128)(2,1)} %copy-done.1), kind=kLoop, calls=%fused_computation.23 | loop fusion | flops 4194304 | bytes 6291456 | tf_op jit(solution)/shard_map/convert_element_type | solution.py:145
  150.0 5.6 %multiply_convert_fusion = bf16[512,448]{0,1:T(8,128)(2,1)S(1)} fusion(bf16[1,4096,448]{1,2,0:T(8,128)(2,1)} %param.17, f32[4096]{0:T(1024)S(1)} %bitcast.89, f32[512]{0:T(512)S(1)} %get-tuple-element.78, bf16[3,512,4096]{2,1,0:T(8,128)(2,1)} %copy-done), kind=kOutput, calls=%fused_computation.36 | convolution fusion | flops 1888583680 | bytes 8341504 | tf_op jit(solution)/shard_map/dot_general | solution.py:198
  156.6 4.4 %convolution_convert_fusion.1 = bf16[512,4096]{1,0:T(8,128)(2,1)S(1)} fusion(bf16[512,448]{1,0:T(8,128)(2,1)S(1)} %bitcast.87, bf16[1,448,4096]{2,1,0:T(8,128)(2,1)} %param.18), kind=kOutput, calls=%fused_computation.16 | convolution fusion | flops 1881145344 | bytes 8323072 | tf_op jit(solution)/shard_map/dot_general | solution.py:204
  161.4 4.0 %collective-permute-done.1 = bf16[256,4096]{1,0:T(8,128)(2,1)S(1)} collective-permute-done((bf16[256,4096]{1,0:T(8,128)(2,1)S(1)}, bf16[256,4096]{1,0:T(8,128)(2,1)S(1)}, u32[]{:S(2)}, u32[]{:S(2)}) %collective-permute-start.1) | collective-permute-done | bytes 2097184 | tf_op jit(solution)/shard_map/ppermute | solution.py:133
  165.4 2.2 add_convert_fusion.1
  171.4 9.1 %fusion.98 = (bf16[1,512,4096]{2,1,0:T(8,128)(2,1)}, bf16[1,512,4096]{2,1,0:T(8,128)(2,1)}, bf16[1,512,4096]{2,1,0:T(8,128)(2,1)}) fusion(bf16[3,512,4096]{2,1,0:T(8,128)(2,1)} %copy-done), kind=kLoop, calls=%fused_computation.268 | loop fusion | bytes 25165824 | tf_op jit(solution)/shard_map/slice | solution.py:213
  180.5 57.4 %reduce-scatter.5.cloned.1.call-done = bf16[16,4096]{1,0:T(8,128)(2,1)} async-done(((bf16[256,4096]{1,0:T(8,128)(2,1)}), bf16[16,4096]{1,0:T(8,128)(2,1)}) %reduce-scatter.5.cloned.1.call-update) | async-done | bytes 131088 | tf_op jit(solution)/shard_map/reduce_scatter | solution.py:146
  240.3 5.9 %collective-permute-start.4 = (bf16[16,4096]{1,0:T(8,128)(2,1)S(1)}, bf16[16,4096]{1,0:T(8,128)(2,1)S(1)}, u32[]{:S(2)}, u32[]{:S(2)}) collective-permute-start(bf16[16,4096]{1,0:T(8,128)(2,1)S(1)} %fusion.41), channel_id=1, source_target_pairs={{8,0},{16,8},{24,16},{32,24},{40,32},{48,40},{56,48},{9,1},{17,9},... | collective-permute-start | bytes 393224 | tf_op jit(solution)/shard_map/ppermute | solution.py:17
  246.1 82.9 %reduce-scatter.3.cloned.1.call-done = bf16[16,4096]{1,0:T(8,128)(2,1)} async-done(((bf16[256,4096]{1,0:T(8,128)(2,1)}), bf16[16,4096]{1,0:T(8,128)(2,1)}) %reduce-scatter.3.cloned.1.call-update) | async-done | bytes 131088 | tf_op jit(solution)/shard_map/reduce_scatter | solution.py:146
  330.1 3.4 collective-permute-start.2
  333.5 5.5 %collective-permute-done.2 = bf16[16,4096]{1,0:T(8,128)(2,1)S(1)} collective-permute-done((bf16[16,4096]{1,0:T(8,128)(2,1)S(1)}, bf16[16,4096]{1,0:T(8,128)(2,1)S(1)}, u32[]{:S(2)}, u32[]{:S(2)}) %collective-permute-start.2) | collective-permute-done | bytes 131104 | tf_op jit(solution)/shard_map/ppermute | solution.py:17
  (111 shorter events, 17.9 us)
Async XLA Ops:
  7.2 102.3 %all-gather.2.cloned.1.call-start = ((), (), s32[]{:S(2)}) async-start(), calls=%async_computation.2 | async-start | bytes 6684672 | tf_op jit(solution)/shard_map/all_gather | solution.py:195
  9.1 228.8 %reduce-scatter.5.cloned.1.call-start = ((), (), s32[]{:S(2)}) async-start(), calls=%async_computation.4 | async-start | bytes 2228224 | tf_op jit(solution)/shard_map/reduce_scatter | solution.py:146
  109.5 10.5 %collective-permute-start = (bf16[3,256,4096]{2,1,0:T(8,128)(2,1)}, bf16[3,256,4096]{2,1,0:T(8,128)(2,1)}, u32[]{:S(2)}, u32[]{:S(2)}) collective-permute-start(bf16[3,256,4096]{2,1,0:T(8,128)(2,1)} %all-gather.2.cloned.1.call-done), channel_id=1, source_target_pairs={{0,1},{1,0},{2,3},{3,2},{4,5},{5,4},{6,7},{7,6},{8,9},{9,8},{10,11... | collective-permute-start | bytes 18874376 | tf_op jit(solution)/shard_map/ppermute | solution.py:133
  123.2 7.0 %copy-start = (bf16[3,512,4096]{2,1,0:T(8,128)(2,1)}, bf16[3,512,4096]{2,1,0:T(8,128)(2,1)S(1)}, u32[]{:S(2)}) copy-start(bf16[3,512,4096]{2,1,0:T(8,128)(2,1)S(1)} %constant_dynamic-update-slice_fusion) | copy-start | bytes 37748740
  123.2 4.8 %copy-start.2 = (bf16[1,4096,448]{1,2,0:T(8,128)(2,1)S(1)}, bf16[1,4096,448]{1,2,0:T(8,128)(2,1)}, u32[]{:S(2)}) copy-start(bf16[1,4096,448]{1,2,0:T(8,128)(2,1)} %param.17) | copy-start | bytes 11010052
  128.0 2.8 copy-start.3
  138.4 2.0 copy-start.1
  141.9 4.4 %collective-permute-start.3 = (bf16[256,4096]{1,0:T(8,128)(2,1)}, bf16[256,4096]{1,0:T(8,128)(2,1)S(1)}, u32[]{:S(2)}, u32[]{:S(2)}) collective-permute-start(bf16[256,4096]{1,0:T(8,128)(2,1)} %slice.133), channel_id=1, source_target_pairs={{0,1},{1,0},{2,3},{3,2},{4,5},{5,4},{6,7},{7,6},{8,9},{9,8},{10,11... | collective-permute-start | bytes 6291464 | tf_op jit(solution)/shard_map/ppermute | solution.py:133
  150.0 179.1 %reduce-scatter.3.cloned.1.call-start = ((), (), s32[]{:S(2)}) async-start(), calls=%async_computation.3 | async-start | bytes 2228224 | tf_op jit(solution)/shard_map/reduce_scatter | solution.py:146
  161.2 4.2 %collective-permute-start.1 = (bf16[256,4096]{1,0:T(8,128)(2,1)S(1)}, bf16[256,4096]{1,0:T(8,128)(2,1)S(1)}, u32[]{:S(2)}, u32[]{:S(2)}) collective-permute-start(bf16[256,4096]{1,0:T(8,128)(2,1)S(1)} %slice.129), channel_id=1, source_target_pairs={{0,1},{1,0},{2,3},{3,2},{4,5},{5,4},{6,7},{7,6},{8,9},{9,8},{10,11... | collective-permute-start | bytes 6291464 | tf_op jit(solution)/shard_map/ppermute | solution.py:133
  240.3 93.2 %collective-permute-start.4 = (bf16[16,4096]{1,0:T(8,128)(2,1)S(1)}, bf16[16,4096]{1,0:T(8,128)(2,1)S(1)}, u32[]{:S(2)}, u32[]{:S(2)}) collective-permute-start(bf16[16,4096]{1,0:T(8,128)(2,1)S(1)} %fusion.41), channel_id=1, source_target_pairs={{8,0},{16,8},{24,16},{32,24},{40,32},{48,40},{56,48},{9,1},{17,9},... | collective-permute-start | bytes 393224 | tf_op jit(solution)/shard_map/ppermute | solution.py:17
  330.1 9.0 %collective-permute-start.2 = (bf16[16,4096]{1,0:T(8,128)(2,1)S(1)}, bf16[16,4096]{1,0:T(8,128)(2,1)S(1)}, u32[]{:S(2)}, u32[]{:S(2)}) collective-permute-start(bf16[16,4096]{1,0:T(8,128)(2,1)S(1)} %fusion.43), channel_id=1, source_target_pairs={{0,8},{8,16},{16,24},{24,32},{32,40},{40,48},{48,56},{1,9},{9,17},... | collective-permute-start | bytes 393224 | tf_op jit(solution)/shard_map/ppermute | solution.py:17
Sparse Core Ops, SparseCore 0:
  10.5 98.9 all-gather.1
  150.1 87.7 reduce-scatter.4
  241.5 87.5 reduce-scatter.2

commit v3 on v2

--- a/solution.py
+++ b/solution.py
@@ -133,19 +133,29 @@
     return lax.ppermute(values, "core", [(0, 1), (1, 0)])
 
 
-def gathered_place(blocks, cores, core_index, per_core):
+def gather_rows(values):
+    group = lax.axis_size("rep") * lax.axis_size("zh")
+    copies = jnp.broadcast_to(values[:, None], (values.shape[0], group) + values.shape[1:])
+    near = lax.all_to_all(copies, ("rep", "zh"), 1, 1, tiled=True)
+    both = jnp.stack([near, swap_cores(near)], axis=1)
+    return both.reshape(values.shape[0], -1, values.shape[-1])
+
+
+def scatter_rows(partial):
+    width = partial.shape[-1]
+    group = lax.axis_size("rep") * lax.axis_size("zh")
+    shaped = partial.reshape(partial.shape[0], 2, group, BLOCK, width)
+    total = shaped[:, 0].astype(jnp.float32) + swap_cores(shaped[:, 1]).astype(jnp.float32)
+    parts = lax.all_to_all(total.astype(jnp.bfloat16), ("rep", "zh"), 1, 1, tiled=True)
+    return jnp.sum(parts.astype(jnp.float32), axis=1)
+
+
+def gathered_place(blocks, core_index):
+    per_core, cores = lax.axis_size("zh"), lax.axis_size("core")
     split = blocks % (cores * per_core)
     spot = (split % cores != core_index) * (lax.axis_size("rep") * per_core)
     spot = spot + (blocks // (cores * per_core)) * per_core + split // cores
     return jnp.where(blocks >= 0, spot, -1)
-
-
-def two_stage_sum(partial, half):
-    mine, theirs = partial[:half], partial[half:]
-    total = (mine.astype(jnp.float32) + swap_cores(theirs).astype(jnp.float32)).astype(jnp.bfloat16)
-    return lax.psum_scatter(total, ("rep", "zh"), scatter_dimension=0, tiled=True).astype(
-        jnp.float32
-    )
 
 
 def local(
@@ -189,26 +199,27 @@
     slot_group = slots % group
     dest = (slot_group // per_core) * (per_core * cores) + (slot_group % per_core) * cores + slot_core
     me = replica_index * (per_core * cores) + zh_index * cores + core_index
-    later_at = gathered_place(later, cores, core_index, per_core)
-    earlier_at = gathered_place(earlier, cores, core_index, per_core)
-    own = jnp.stack([act_forward[0, 0], act_saved[0, 0], grad_output[0, 0]])
-    near = lax.all_gather(own, ("rep", "zh"), axis=1, tiled=True)
-    every = jnp.concatenate([near, swap_cores(near)], axis=1)
+    later_at = gathered_place(later, core_index)
+    earlier_at = gathered_place(earlier, core_index)
+    fresh_every = gather_rows(act_forward[0])
+    pair, fresh_every = lax.optimization_barrier(
+        (jnp.stack([act_saved[0, 0], grad_output[0, 0]]), fresh_every)
+    )
+    saved_every, upstream_every = gather_rows(pair)
+    every = (fresh_every[0], saved_every, upstream_every)
     hidden = jax.nn.silu(
         jnp.dot(normalize(every[0], gain_row), w_up, preferred_element_type=jnp.float32)
     ).astype(jnp.bfloat16)
     upper = jnp.dot(normalize(every[1], gain_row), w_up, preferred_element_type=jnp.float32)
     back_hidden = (against_rows(every[2], w_down) * silu_slope(upper)).astype(jnp.bfloat16)
-    half = group * local_rows
-    mixed = two_stage_sum(
+    mixed = scatter_rows(
         jnp.dot(pick_blocks(hidden, later_at[dest]), w_down, preferred_element_type=jnp.float32).astype(
             jnp.bfloat16
-        ),
-        half,
-    )
-    returned = two_stage_sum(
-        against_rows(pick_blocks(back_hidden, earlier_at[dest]), w_up).astype(jnp.bfloat16), half
-    )
+        )[None]
+    )[0]
+    returned = scatter_rows(
+        against_rows(pick_blocks(back_hidden, earlier_at[dest]), w_up).astype(jnp.bfloat16)[None]
+    )[0]
     fresh_mine = pick_blocks(every[0], later_at[me][None])
     saved_mine = pick_blocks(every[1], earlier_at[me][None])
     upstream_mine = pick_blocks(every[2], earlier_at[me][None])

time: 347 us -> 326 us (0.939)
  waiting for transfers between devices: 251 us -> 211 us
  starting transfers between devices: 9.77 us -> 41.5 us
  between operations: 16.7 us -> 3.8 us
  local copies, waits for them, and re-layouts: 32.1 us -> 20.1 us
  other arithmetic: 18.5 us -> 29 us
    all_to_all x0 -> x4, waiting for transfers between devices: none -> 201 us  [the longest x2 135 us: gather_rows(): near = lax.all_to_all(copies, ('rep', 'zh'), 1, 1, tiled=True)]
    reduce_scatter x2 -> x0, waiting for transfers between devices: 140 us -> none  [two_stage_sum(): lax.psum_scatter(total, ('rep', 'zh'), scatter_dimension=0, tiled=True)]
    all_gather x1 -> x0, waiting for transfers between devices: 97.1 us -> none  [local(): near = lax.all_gather(own, ('rep', 'zh'), axis=1, tiled=True)]
    all_to_all x0 -> x4, starting transfers between devices: none -> 31.1 us  [the longest x2 16.1 us: scatter_rows(): lax.all_to_all(total.astype(jnp.bfloat16), ('rep', 'zh'), 1, 1, tiled=True)]
    slice x3 -> x0, local copies, waits for them, and re-layouts: 10.8 us -> none  [the longest x1 9.14 us: local(): saved_mine = pick_blocks(every[1], earlier_at[me][None])]
    reduce_sum x1 -> x2, other arithmetic: 1.8 us -> 7.82 us  [normalize(): scale = lax.rsqrt(jnp.mean(wide * wide, axis=-1, keepdims=True) + EPSILON)]
    broadcast_in_dim x0 -> x2, local copies, waits for them, and re-layouts: none -> 5.02 us  [gather_rows(): jnp.broadcast_to(values[:, None], (values.shape[0], group) + values.shape...]
    unnamed x11 -> x26, local copies, waits for them, and re-layouts: 10 us -> 5.36 us
  transfers between devices with their start and end apart: 8 -> 10, of which waited for: 7 -> 8; matrix products, arithmetic and copies ran while one was open for 12% -> 17% of each run, Pallas kernels for 0% -> 0%
where the time goes in v3:
time: 326 us; the launch traced here: 323 us
  waiting for transfers between devices  211 us (65%)
  starting transfers between devices  41.5 us (13%)
  other arithmetic  29 us (9%)
  local copies, waits for them, and re-layouts  20.1 us (6%)
  matrix products  17.5 us (5%)
  between operations  3.8 us (1%)
    all_to_all x2, waiting for transfers between devices, gather_rows(): near = lax.all_to_all(copies, ('rep', 'zh'), 1, 1, tiled=True)  135 us
    all_to_all x2, waiting for transfers between devices, scatter_rows(): lax.all_to_all(total.astype(jnp.bfloat16), ('rep', 'zh'), 1, 1, tiled=True)  65.4 us
    all_to_all x2, starting transfers between devices, scatter_rows(): lax.all_to_all(total.astype(jnp.bfloat16), ('rep', 'zh'), 1, 1, tiled=True)  16.1 us
    all_to_all x2, starting transfers between devices, gather_rows(): near = lax.all_to_all(copies, ('rep', 'zh'), 1, 1, tiled=True)  15 us
    ppermute x2, starting transfers between devices, from_behind(): return lax.ppermute(block, axis, route)  9.66 us
    reduce_sum x2, other arithmetic, normalize(): scale = lax.rsqrt(jnp.mean(wide * wide, axis=-1, keepdims=True) + EPSILON)  7.82 us
    ppermute x4, waiting for transfers between devices, swap_cores(): return lax.ppermute(values, 'core', [(0, 1), (1, 0)])  7.75 us
    dot_general x2, matrix products, against_rows(): lax.dot_general(left, right, (((1,), (1,)), ((), ())), preferred_element_...  6.62 us
  transfers between devices with their start and end apart: 10, of which 8 were waited for; matrix products, arithmetic and copies ran while one was open for 17% of the time, Pallas kernels for 0%

profile of v3, /device:TPU:32, one launch (start us, length us, event | category | flops | bytes accessed | tf_op | source)
XLA Modules:
  0.0 322.8 jit_solution(12980979127095603506)
XLA Ops:
  0.7 2.5 broadcast_in_dim.331
  3.2 10.3 %all-to-all-start = ((bf16[1,16,16,4096]{3,2,0,1:T(8,128)(2,1)}), bf16[1,16,16,4096]{3,2,0,1:T(8,128)(2,1)S(1)}, u32[]{:S(2)}, u32[]{:S(2)}) async-start(bf16[1,16,16,4096]{3,2,0,1:T(8,128)(2,1)} %broadcast_in_dim.331), calls=%async_computation | async-start | bytes 4194304 | tf_op jit(solution)/shard_map/all_to_all | solution.py:139
  13.8 51.9 %all-to-all-done = bf16[1,16,16,4096]{3,2,0,1:T(8,128)(2,1)S(1)} async-done(((bf16[1,16,16,4096]{3,2,0,1:T(8,128)(2,1)}), bf16[1,16,16,4096]{3,2,0,1:T(8,128)(2,1)S(1)}, u32[]{:S(2)}, u32[]{:S(2)}) %all-to-all-start) | async-done | bytes 2097184 | tf_op jit(solution)/shard_map/all_to_all | solution.py:139
  66.7 3.2 collective-permute-done
  69.9 2.3 pad_maximum_fusion.1
  72.1 2.5 broadcast_in_dim.346
  74.6 4.7 %all-to-all-start.2 = ((bf16[2,16,16,4096]{3,2,0,1:T(8,128)(2,1)}), bf16[2,16,16,4096]{3,2,0,1:T(8,128)(2,1)}, u32[]{:S(2)}, u32[]{:S(2)}) async-start(bf16[2,16,16,4096]{3,2,0,1:T(8,128)(2,1)} %broadcast_in_dim.346), calls=%async_computation.2 | async-start | bytes 8388608 | tf_op jit(solution)/shard_map/all_to_all | solution.py:139
  83.3 3.2 %fusion = f32[512]{0:T(512)S(1)} fusion(bf16[1,512,4096]{2,1,0:T(8,128)(2,1)} %bitcast.104), kind=kLoop, calls=%fused_computation.9 | loop fusion | flops 6290944 | bytes 4196352 | tf_op jit(solution)/shard_map/reduce_sum | solution.py:96
  86.8 4.3 %multiply_convert_fusion = bf16[512,448]{0,1:T(8,128)(2,1)S(1)} fusion(bf16[1,4096,448]{1,2,0:T(8,128)(2,1)} %param.17, bf16[1,512,4096]{2,1,0:T(8,128)(2,1)S(1)} %bitcast.106, f32[4096]{0:T(1024)S(1)} %bitcast.120, f32[512]{0:T(512)S(1)} %add_rsqrt_fusion.1), kind=kOutput, calls=%fused_computation.45 | convolution fusion | flops 1888583680 | bytes 8341504 | tf_op jit(solution)/shard_map/dot_general | solution.py:211
  92.1 83.4 %all-to-all-done.2 = bf16[2,16,16,4096]{3,2,0,1:T(8,128)(2,1)} async-done(((bf16[2,16,16,4096]{3,2,0,1:T(8,128)(2,1)}), bf16[2,16,16,4096]{3,2,0,1:T(8,128)(2,1)}, u32[]{:S(2)}, u32[]{:S(2)}) %all-to-all-start.2) | async-done | bytes 4194336 | tf_op jit(solution)/shard_map/all_to_all | solution.py:139
  175.5 4.4 %convolution_convert_fusion.1 = bf16[512,4096]{1,0:T(8,128)(2,1)S(1)} fusion(bf16[512,448]{1,0:T(8,128)(2,1)S(1)} %bitcast.118, bf16[1,448,4096]{2,1,0:T(8,128)(2,1)} %param.18), kind=kOutput, calls=%fused_computation.18 | convolution fusion | flops 1881145344 | bytes 8323072 | tf_op jit(solution)/shard_map/dot_general | solution.py:216
  184.1 2.4 scatter_custom_fusion
  187.9 3.7 %fusion.11 = bf16[1,16,16,4096]{3,2,0,1:T(8,128)(2,1)} fusion(bf16[1,16,16,4096]{3,2,0,1:T(8,128)(2,1)S(1)} %collective-permute-done.1, bf16[1,2,16,16,4096]{4,3,2,1,0:T(8,128)(2,1)} %bitcast.111), kind=kLoop, calls=%fused_computation.27 | loop fusion | flops 4194304 | bytes 6291456 | tf_op jit(solution)/shard_map/convert_element_type | solution.py:149
  191.6 10.9 %all-to-all-start.1 = ((bf16[1,16,16,4096]{3,2,0,1:T(8,128)(2,1)}), bf16[1,16,16,4096]{3,2,0,1:T(8,128)(2,1)S(1)}, u32[]{:S(2)}, u32[]{:S(2)}) async-start(bf16[1,16,16,4096]{3,2,0,1:T(8,128)(2,1)} %fusion.11), calls=%async_computation.1 | async-start | bytes 4194304 | tf_op jit(solution)/shard_map/all_to_all | solution.py:149
  202.5 2.4 fusion.6
  205.0 4.6 %fusion.3 = (f32[2,16,16]{2,1,0:T(8,128)S(1)}, bf16[1,2,16,16,4096]{4,3,0,2,1:T(8,128)(2,1)S(1)}) fusion(bf16[2,1,16,16,4096]{4,3,0,2,1:T(8,128)(2,1)} %bitcast.36, bf16[2,1,16,16,4096]{4,3,0,2,1:T(8,128)(2,1)} %bitcast.35), kind=kLoop, calls=%fused_computation.12 | loop fusion | flops 8388096 | bytes 12584960 | tf_op jit(solution)/shard_map/reduce_sum | solution.py:96
  218.4 4.4 %convolution_convert_fusion = bf16[512,4096]{1,0:T(8,128)(2,1)S(1)} fusion(bf16[512,448]{1,0:T(8,128)(2,1)S(1)} %bitcast.119, bf16[1,4096,448]{1,2,0:T(8,128)(2,1)} %param.17), kind=kOutput, calls=%fused_computation.17 | convolution fusion | flops 1881145344 | bytes 8323072 | tf_op jit(solution)/shard_map/dot_general | solution.py:115
  223.1 4.1 %collective-permute-done.4 = bf16[1,16,16,4096]{3,2,0,1:T(8,128)(2,1)S(1)} collective-permute-done((bf16[1,16,16,4096]{3,2,0,1:T(8,128)(2,1)S(1)}, bf16[1,16,16,4096]{3,2,0,1:T(8,128)(2,1)S(1)}, u32[]{:S(2)}, u32[]{:S(2)}) %collective-permute-start.4) | collective-permute-done | bytes 2097184 | tf_op jit(solution)/shard_map/ppermute | solution.py:133
  229.4 21.9 %all-to-all-done.1 = bf16[1,16,16,4096]{3,2,0,1:T(8,128)(2,1)S(1)} async-done(((bf16[1,16,16,4096]{3,2,0,1:T(8,128)(2,1)}), bf16[1,16,16,4096]{3,2,0,1:T(8,128)(2,1)S(1)}, u32[]{:S(2)}, u32[]{:S(2)}) %all-to-all-start.1) | async-done | bytes 2097184 | tf_op jit(solution)/shard_map/all_to_all | solution.py:149
  251.3 5.3 %all-to-all-start.3 = ((bf16[1,16,16,4096]{3,2,0,1:T(8,128)(2,1)}), bf16[1,16,16,4096]{3,2,0,1:T(8,128)(2,1)}, u32[]{:S(2)}, u32[]{:S(2)}) async-start(bf16[1,16,16,4096]{3,2,0,1:T(8,128)(2,1)} %fusion.10), calls=%async_computation.3 | async-start | bytes 4194304 | tf_op jit(solution)/shard_map/all_to_all | solution.py:149
  261.6 3.4 %collective-permute-start.2 = (bf16[16,4096]{1,0:T(8,128)(2,1)S(1)}, bf16[16,4096]{1,0:T(8,128)(2,1)S(1)}, u32[]{:S(2)}, u32[]{:S(2)}) collective-permute-start(bf16[16,4096]{1,0:T(8,128)(2,1)S(1)} %fusion.37), channel_id=1, source_target_pairs={{0,8},{8,16},{16,24},{24,32},{32,40},{40,48},{48,56},{1,9},{9,17},... | collective-permute-start | bytes 393224 | tf_op jit(solution)/shard_map/ppermute | solution.py:17
  265.0 43.5 %all-to-all-done.3 = bf16[1,16,16,4096]{3,2,0,1:T(8,128)(2,1)} async-done(((bf16[1,16,16,4096]{3,2,0,1:T(8,128)(2,1)}), bf16[1,16,16,4096]{3,2,0,1:T(8,128)(2,1)}, u32[]{:S(2)}, u32[]{:S(2)}) %all-to-all-start.3) | async-done | bytes 2097184 | tf_op jit(solution)/shard_map/all_to_all | solution.py:149
  312.7 6.3 %collective-permute-start.5 = (bf16[16,4096]{1,0:T(8,128)(2,1)S(1)}, bf16[16,4096]{1,0:T(8,128)(2,1)S(1)}, u32[]{:S(2)}, u32[]{:S(2)}) collective-permute-start(bf16[16,4096]{1,0:T(8,128)(2,1)S(1)} %fusion.35), channel_id=1, source_target_pairs={{8,0},{16,8},{24,16},{32,24},{40,32},{48,40},{56,48},{9,1},{17,9},... | collective-permute-start | bytes 393224 | tf_op jit(solution)/shard_map/ppermute | solution.py:17
  318.9 2.5 collective-permute-done.5
  (134 shorter events, 30.9 us)
Async XLA Ops:
  0.6 12.9 %copy-start.11 = (s32[4]{0:T(128)S(1)}, s32[4]{0:T(128)}, u32[]{:S(2)}) copy-start(s32[4]{0:T(128)} %param.19) | copy-start | bytes 52
  0.6 65.1 %copy-start.7 = (s32[3,4]{1,0:T(4,128)S(1)}, s32[3,4]{1,0:T(4,128)}, u32[]{:S(2)}) copy-start(s32[3,4]{1,0:T(4,128)} %param.21) | copy-start | bytes 148
  0.7 65.1 %copy-start.8 = (s32[3,4]{1,0:T(4,128)S(1)}, s32[3,4]{1,0:T(4,128)}, u32[]{:S(2)}) copy-start(s32[3,4]{1,0:T(4,128)} %param.20) | copy-start | bytes 148
  0.7 65.9 %copy-start.4 = (bf16[1,1,16,4096]{3,2,1,0:T(8,128)(2,1)S(1)}, bf16[1,1,16,4096]{3,2,1,0:T(8,128)(2,1)}, u32[]{:S(2)}) copy-start(bf16[1,1,16,4096]{3,2,1,0:T(8,128)(2,1)} %param.15) | copy-start | bytes 393220
  0.7 65.9 %copy-start.5 = (bf16[1,1,16,4096]{3,2,1,0:T(8,128)(2,1)S(1)}, bf16[1,1,16,4096]{3,2,1,0:T(8,128)(2,1)}, u32[]{:S(2)}) copy-start(bf16[1,1,16,4096]{3,2,1,0:T(8,128)(2,1)} %param.14) | copy-start | bytes 393220
  3.2 62.5 %all-to-all-start = ((bf16[1,16,16,4096]{3,2,0,1:T(8,128)(2,1)}), bf16[1,16,16,4096]{3,2,0,1:T(8,128)(2,1)S(1)}, u32[]{:S(2)}, u32[]{:S(2)}) async-start(bf16[1,16,16,4096]{3,2,0,1:T(8,128)(2,1)} %broadcast_in_dim.331), calls=%async_computation | async-start | bytes 4194304 | tf_op jit(solution)/shard_map/all_to_all | solution.py:139
  65.7 4.2 %collective-permute-start = (bf16[1,16,16,4096]{3,2,0,1:T(8,128)(2,1)S(1)}, bf16[1,16,16,4096]{3,2,0,1:T(8,128)(2,1)S(1)}, u32[]{:S(2)}, u32[]{:S(2)}) collective-permute-start(bf16[1,16,16,4096]{3,2,0,1:T(8,128)(2,1)S(1)} %all-to-all-done), channel_id=1, source_target_pairs={{0,1},{1,0},{2,3},{3,2},{4,5},{5,4},{6,7},{7,6},{8,9},{9,8},{10,11... | collective-permute-start | bytes 6291464 | tf_op jit(solution)/shard_map/ppermute | solution.py:133
  74.6 7.9 %copy-start.6 = (bf16[1,4096]{1,0:T(2,128)(2,1)S(1)}, bf16[1,4096]{1,0:T(2,128)(2,1)}, u32[]{:S(2)}) copy-start(bf16[1,4096]{1,0:T(2,128)(2,1)} %param.16) | copy-start | bytes 24580
  74.6 100.8 %all-to-all-start.2 = ((bf16[2,16,16,4096]{3,2,0,1:T(8,128)(2,1)}), bf16[2,16,16,4096]{3,2,0,1:T(8,128)(2,1)}, u32[]{:S(2)}, u32[]{:S(2)}) async-start(bf16[2,16,16,4096]{3,2,0,1:T(8,128)(2,1)} %broadcast_in_dim.346), calls=%async_computation.2 | async-start | bytes 8388608 | tf_op jit(solution)/shard_map/all_to_all | solution.py:139
  83.3 3.5 %copy-start.1 = (bf16[1,2,16,16,4096]{4,3,2,1,0:T(8,128)(2,1)S(1)}, bf16[1,2,16,16,4096]{4,3,2,1,0:T(8,128)(2,1)}, u32[]{:S(2)}) copy-start(bf16[1,2,16,16,4096]{4,3,2,1,0:T(8,128)(2,1)} %pad_maximum_fusion.1) | copy-start | bytes 12582916
  175.5 27.1 %collective-permute-start.3 = (bf16[2,16,16,4096]{3,2,0,1:T(8,128)(2,1)}, bf16[2,16,16,4096]{3,2,0,1:T(8,128)(2,1)}, u32[]{:S(2)}, u32[]{:S(2)}) collective-permute-start(bf16[2,16,16,4096]{3,2,0,1:T(8,128)(2,1)} %all-to-all-done.2), channel_id=1, source_target_pairs={{0,1},{1,0},{2,3},{3,2},{4,5},{5,4},{6,7},{7,6},{8,9},{9,8},{10,11... | collective-permute-start | bytes 12582920 | tf_op jit(solution)/shard_map/ppermute | solution.py:133
  179.9 2.0 copy-start.3
  183.4 4.5 %collective-permute-start.1 = (bf16[1,16,16,4096]{3,2,0,1:T(8,128)(2,1)}, bf16[1,16,16,4096]{3,2,0,1:T(8,128)(2,1)S(1)}, u32[]{:S(2)}, u32[]{:S(2)}) collective-permute-start(bf16[1,16,16,4096]{3,2,0,1:T(8,128)(2,1)} %slice_bitcast_fusion.2), channel_id=1, source_target_pairs={{0,1},{1,0},{2,3},{3,2},{4,5},{5,4},{6,7},{7,6},{8,9},{9,8},{10,11... | collective-permute-start | bytes 6291464 | tf_op jit(solution)/shard_map/ppermute | solution.py:133
  191.6 59.6 %all-to-all-start.1 = ((bf16[1,16,16,4096]{3,2,0,1:T(8,128)(2,1)}), bf16[1,16,16,4096]{3,2,0,1:T(8,128)(2,1)S(1)}, u32[]{:S(2)}, u32[]{:S(2)}) async-start(bf16[1,16,16,4096]{3,2,0,1:T(8,128)(2,1)} %fusion.11), calls=%async_computation.1 | async-start | bytes 4194304 | tf_op jit(solution)/shard_map/all_to_all | solution.py:149
  204.9 10.3 %copy-start.2 = (bf16[1,2,16,16,4096]{4,3,0,2,1:T(8,128)(2,1)}, bf16[1,2,16,16,4096]{4,3,0,2,1:T(8,128)(2,1)S(1)}, u32[]{:S(2)}) copy-start(bf16[1,2,16,16,4096]{4,3,0,2,1:T(8,128)(2,1)S(1)} %fusion.6) | copy-start | bytes 12582916
  209.6 2.1 copy-start
  209.6 3.5 %copy-start.10 = (bf16[1,4096,448]{1,2,0:T(8,128)(2,1)S(1)}, bf16[1,4096,448]{1,2,0:T(8,128)(2,1)}, u32[]{:S(2)}) copy-start(bf16[1,4096,448]{1,2,0:T(8,128)(2,1)} %param.17) | copy-start | bytes 11010052
  213.1 2.1 copy-start.9
  223.0 4.2 %collective-permute-start.4 = (bf16[1,16,16,4096]{3,2,0,1:T(8,128)(2,1)S(1)}, bf16[1,16,16,4096]{3,2,0,1:T(8,128)(2,1)S(1)}, u32[]{:S(2)}, u32[]{:S(2)}) collective-permute-start(bf16[1,16,16,4096]{3,2,0,1:T(8,128)(2,1)S(1)} %slice_bitcast_fusion), channel_id=1, source_target_pairs={{0,1},{1,0},{2,3},{3,2},{4,5},{5,4},{6,7},{7,6},{8,9},{9,8},{10,11... | collective-permute-start | bytes 6291464 | tf_op jit(solution)/shard_map/ppermute | solution.py:133
  251.3 57.2 %all-to-all-start.3 = ((bf16[1,16,16,4096]{3,2,0,1:T(8,128)(2,1)}), bf16[1,16,16,4096]{3,2,0,1:T(8,128)(2,1)}, u32[]{:S(2)}, u32[]{:S(2)}) async-start(bf16[1,16,16,4096]{3,2,0,1:T(8,128)(2,1)} %fusion.10), calls=%async_computation.3 | async-start | bytes 4194304 | tf_op jit(solution)/shard_map/all_to_all | solution.py:149
  261.6 57.3 %collective-permute-start.2 = (bf16[16,4096]{1,0:T(8,128)(2,1)S(1)}, bf16[16,4096]{1,0:T(8,128)(2,1)S(1)}, u32[]{:S(2)}, u32[]{:S(2)}) collective-permute-start(bf16[16,4096]{1,0:T(8,128)(2,1)S(1)} %fusion.37), channel_id=1, source_target_pairs={{0,8},{8,16},{16,24},{24,32},{32,40},{40,48},{48,56},{1,9},{9,17},... | collective-permute-start | bytes 393224 | tf_op jit(solution)/shard_map/ppermute | solution.py:17
  312.7 8.8 %collective-permute-start.5 = (bf16[16,4096]{1,0:T(8,128)(2,1)S(1)}, bf16[16,4096]{1,0:T(8,128)(2,1)S(1)}, u32[]{:S(2)}, u32[]{:S(2)}) collective-permute-start(bf16[16,4096]{1,0:T(8,128)(2,1)S(1)} %fusion.35), channel_id=1, source_target_pairs={{8,0},{16,8},{24,16},{32,24},{40,32},{48,40},{56,48},{9,1},{17,9},... | collective-permute-start | bytes 393224 | tf_op jit(solution)/shard_map/ppermute | solution.py:17
